TPU v7x, 256 devices: a whole 4x4x8 slice. The times are simulated.
256 devices in a mesh: dp: 32 (over z, x_hi, core), tm: 8 (over y, x_lo).
Axes of the slice: x: 4 (x_hi: 2, x_lo: 2; x = x_hi * 2 + x_lo), y: 4, z: 8, core: 2. Of those that a mesh axis runs over, the one named last changes fastest.
Arguments:
- queries: bfloat16 [32, 3072, 256], P('dp', 'tm'), may hold values from -6 to 6
- key_input: bfloat16 [32, 3072, 256], P('dp', 'tm'), may hold values from -6 to 6
- value_input: bfloat16 [32, 3072, 256], P('dp', 'tm'), may hold values from -6 to 6
- lengths: int32 [32], P('dp'), may hold values from 1536 to 3072, as said below
- projection: bfloat16 [4096, 256], P('dp'), may hold values from -0.09375 to 0.09375
- upstream: bfloat16 [32, 3072, 4096], P('dp', 'tm'), may hold values from -6 to 6
- glu_input: bfloat16 [32, 3072, 4096], P('dp', 'tm'), may hold values from -6 to 6
- kernel: bfloat16 [2048, 31], P('dp'), may hold values from -1 to 1
- norm_gain: bfloat16 [2048], P('dp'), may hold values from 0.5 to 1.5
- conv_upstream: bfloat16 [32, 3072, 2048], P('dp', 'tm'), may hold values from -6 to 6
Outputs:
- grad_queries: bfloat16 [32, 3072, 256], P('dp', 'tm')
- grad_keys: bfloat16 [32, 3072, 256], P('dp', 'tm')
- grad_values: bfloat16 [32, 3072, 256], P('dp', 'tm')
- grad_projection: bfloat16 [4096, 256], P('dp')
- grad_glu: bfloat16 [32, 3072, 4096], P('dp', 'tm')
- grad_kernel: float32 [2048, 31], P('dp')
- grad_gain: float32 [2048], P('dp')
Inputs may be any that keep to these rules, and one draw needn't show every extreme that they name: `lengths`: the valid frames of an utterance are its first ones; one utterance has all 3072 valid and one exactly 1536.
All inputs are finite; a program needn't handle non-finite values.
Results may differ from a plain program's by a relative error of at most 0.02.
Values may be sent and summed in bfloat16 or wider, within the bound.
No kernel may reach another device: no remote copies, remote signals or barrier semaphores. Data moves between devices by JAX's collectives and lax.ppermute only.
A program may use at most 128 MiB of HBM per device.

v0:
```python
import jax
import jax.numpy as jnp
from jax import lax
from jax.sharding import PartitionSpec as P

HEADS = 2
HDIM = 128
CH = 2048
KW = 31
NEG_FILL = -1e30
NORM_EPS = 1e-05


def from_behind(block, axis, distance):
    devices = range(lax.axis_size(axis))
    route = [((i - distance) % len(devices), i) for i in devices]
    return lax.ppermute(block, axis, route)


def extended(cells, sides, width):
    for axis, dim in sides:
        count = lax.axis_size(axis)
        ends = count - 1
        head = lax.slice_in_dim(cells, 0, width, axis=dim)
        tail = lax.slice_in_dim(cells, cells.shape[dim] - width, cells.shape[dim], axis=dim)
        cells = jnp.concatenate(
            [
                lax.ppermute(tail, axis, [(i, (i + 1) % count) for i in range(ends)]),
                cells,
                lax.ppermute(head, axis, [((i + 1) % count, i) for i in range(ends)]),
            ],
            axis=dim,
        )
    return cells


def depthwise(padded, kernel_f, frame_rows):
    mixed = jnp.zeros((frame_rows, kernel_f.shape[0]), jnp.float32)
    for tap in range(kernel_f.shape[1]):
        mixed = mixed + padded[tap : tap + frame_rows].astype(jnp.float32) * kernel_f[:, tap]
    return mixed


def back_depthwise(grad_pad, kernel_f, frame_rows):
    half_width = (kernel_f.shape[1] - 1) // 2
    result = jnp.zeros((frame_rows, kernel_f.shape[0]), jnp.float32)
    for tap in range(kernel_f.shape[1]):
        begin = 2 * half_width - tap
        result = (
            result + grad_pad[begin : begin + frame_rows].astype(jnp.float32) * kernel_f[:, tap]
        )
    return result


def tap_products(grad_low, padded, frame_rows, tap_count):
    grad_f = grad_low.astype(jnp.float32)
    return jnp.stack(
        [
            jnp.sum(grad_f * padded[tap : tap + frame_rows].astype(jnp.float32), axis=0)
            for tap in range(tap_count)
        ],
        axis=1,
    )


def norm_backward(mixed, gain_f, cotangent, frame_live):
    centre = mixed - jnp.mean(mixed, axis=-1, keepdims=True)
    inv_std = lax.rsqrt(jnp.mean(centre * centre, axis=-1, keepdims=True) + NORM_EPS)
    standard = centre * inv_std
    normed = standard * gain_f
    squash = jax.nn.sigmoid(normed)
    grad_normed = (
        cotangent.astype(jnp.float32) * frame_live * (squash + normed * squash * (1.0 - squash))
    )
    gain_term = jnp.sum(grad_normed * standard, axis=0)
    scaled = grad_normed * gain_f
    grad_conv = inv_std * (
        scaled
        - jnp.mean(scaled, axis=-1, keepdims=True)
        - standard * jnp.mean(scaled * standard, axis=-1, keepdims=True)
    )
    return (grad_conv.astype(jnp.bfloat16), gain_term)


def gather_params(projection, kernel, norm_gain):
    width = projection.shape[1]
    tail = jnp.concatenate([kernel.reshape(-1), norm_gain.reshape(-1)])
    tail_rows = -(-tail.shape[0] // width)
    tail = jnp.pad(tail, (0, tail_rows * width - tail.shape[0])).reshape(tail_rows, width)
    block = jnp.concatenate([projection, tail], axis=0)
    full = lax.all_gather(block, "dp", axis=0, tiled=False)
    count = full.shape[0]
    proj_rows = projection.shape[0]
    full_proj = full[:, :proj_rows].reshape(count * proj_rows, width)
    flat_tail = full[:, proj_rows:].reshape(count, tail_rows * width)
    kernel_size = kernel.shape[0] * kernel.shape[1]
    full_kernel = flat_tail[:, :kernel_size].reshape(count * kernel.shape[0], kernel.shape[1])
    full_gain = flat_tail[:, kernel_size : kernel_size + norm_gain.shape[0]].reshape(-1)
    return (full_proj, full_kernel, full_gain)


def reduce_grads(proj_term, kernel_term, gain_term):
    count = lax.axis_size("dp")
    width = proj_term.shape[1]
    proj_part = lax.psum_scatter(proj_term, "dp", scatter_dimension=0, tiled=True)
    kernel_blocks = kernel_term.reshape(count, -1)
    gain_blocks = gain_term.reshape(count, -1)
    tail = jnp.concatenate([kernel_blocks, gain_blocks], axis=1)
    tail_cols = tail.shape[1]
    tail_rows = -(-tail_cols // width)
    tail = jnp.pad(tail, ((0, 0), (0, tail_rows * width - tail_cols))).reshape(-1, width)
    tail_part = lax.psum_scatter(tail, "dp", scatter_dimension=0, tiled=True)
    total = lax.psum(jnp.concatenate([proj_part, tail_part], axis=0), "tm")
    proj_rows = proj_part.shape[0]
    proj_total = total[:proj_rows]
    flat_tail = total[proj_rows:].reshape(-1)
    kernel_size = kernel_blocks.shape[1]
    kernel_total = flat_tail[:kernel_size].reshape(-1, kernel_term.shape[1])
    gain_total = flat_tail[kernel_size : kernel_size + gain_blocks.shape[1]]
    return (proj_total, kernel_total, gain_total)


def split_three(values):
    high = lax.optimization_barrier(values.astype(jnp.bfloat16))
    rest = values - high.astype(jnp.float32)
    middle = lax.optimization_barrier(rest.astype(jnp.bfloat16))
    low = (rest - middle.astype(jnp.float32)).astype(jnp.bfloat16)
    return jnp.concatenate([high, middle, low], axis=0)


def join_three(parts):
    third = parts.shape[0] // 3
    wide = parts.astype(jnp.float32)
    return wide[:third] + wide[third : 2 * third] + wide[2 * third :]


def per_device(
    queries,
    key_input,
    value_input,
    lengths,
    projection,
    upstream,
    glu_input,
    kernel,
    norm_gain,
    conv_upstream,
):
    time_count = lax.axis_size("tm")
    time_rank = lax.axis_index("tm")
    frame_rows = queries.shape[1]
    flat_width = queries.shape[2]
    score_scale = HDIM ** (-0.5)
    length = lengths[0]
    full_proj, full_kernel, full_gain = gather_params(projection, kernel, norm_gain)
    query_heads = queries[0].reshape(frame_rows, HEADS, HDIM)
    key_own = key_input[0].reshape(frame_rows, HEADS, HDIM)
    value_own = value_input[0].reshape(frame_rows, HEADS, HDIM)
    key_value = lax.all_gather(
        jnp.concatenate([key_input[0], value_input[0]], axis=1), "tm", axis=0, tiled=True
    )
    total_frames = key_value.shape[0]
    key_all = key_value[:, :flat_width].reshape(total_frames, HEADS, HDIM)
    value_all = key_value[:, flat_width:].reshape(total_frames, HEADS, HDIM)
    key_live = jnp.arange(total_frames, dtype=jnp.int32) < length
    scores = (
        jnp.einsum("qhd,khd->hqk", query_heads, key_all, preferred_element_type=jnp.float32)
        * score_scale
    )
    scores = jnp.where(key_live[None, None, :], scores, NEG_FILL)
    row_top = jnp.max(scores, axis=-1)
    log_total = row_top + jnp.log(jnp.sum(jnp.exp(scores - row_top[:, :, None]), axis=-1))
    weights = jnp.exp(scores - log_total[:, :, None])
    weights_high = lax.optimization_barrier(weights.astype(jnp.bfloat16))
    weights_rest = (weights - weights_high.astype(jnp.float32)).astype(jnp.bfloat16)
    attended = (
        jnp.einsum("hqk,khd->qhd", weights_high, value_all, preferred_element_type=jnp.float32)
        + jnp.einsum("hqk,khd->qhd", weights_rest, value_all, preferred_element_type=jnp.float32)
    ).astype(jnp.bfloat16)
    upstream_rows = upstream[0]
    grad_out = jnp.dot(upstream_rows, full_proj, preferred_element_type=jnp.float32).astype(
        jnp.bfloat16
    )
    grad_heads = grad_out.reshape(frame_rows, HEADS, HDIM)
    row_delta = jnp.einsum("qhd,qhd->hq", grad_heads, attended, preferred_element_type=jnp.float32)
    grad_weights = jnp.einsum(
        "qhd,khd->hqk", grad_heads, value_all, preferred_element_type=jnp.float32
    )
    grad_scores = (weights * (grad_weights - row_delta[:, :, None]) * score_scale).astype(
        jnp.bfloat16
    )
    query_acc = jnp.einsum("hqk,khd->qhd", grad_scores, key_all, preferred_element_type=jnp.float32)
    stat_parts = split_three(jnp.concatenate([log_total, row_delta], axis=0))
    pair_width = 2 * flat_width
    stat_rows = -(-stat_parts.size // pair_width)
    stat_rows = -(-stat_rows // 16) * 16
    stat_block = jnp.pad(stat_parts.reshape(-1), (0, stat_rows * pair_width - stat_parts.size))
    packed_rows = jnp.concatenate(
        [
            jnp.concatenate([queries[0], grad_out], axis=1),
            stat_block.reshape(stat_rows, pair_width),
        ],
        axis=0,
    )
    query_grad = lax.all_gather(packed_rows, "tm", axis=0, tiled=False)
    query_pairs = query_grad[:, :frame_rows].reshape(total_frames, pair_width)
    stat_all = query_grad[:, frame_rows:].reshape(time_count, -1)[:, : stat_parts.size]
    stat_all = stat_all.reshape(time_count, stat_parts.shape[0], frame_rows)
    stat_all = join_three(jnp.transpose(stat_all, (1, 0, 2)).reshape(stat_parts.shape[0], -1))
    query_all = query_pairs[:, :flat_width].reshape(total_frames, HEADS, HDIM)
    grad_all = query_pairs[:, flat_width:].reshape(total_frames, HEADS, HDIM)
    log_total_all = stat_all[:HEADS]
    row_delta_all = stat_all[HEADS:]
    own_live = time_rank * frame_rows + jnp.arange(frame_rows, dtype=jnp.int32) < length
    scores_k = (
        jnp.einsum("qhd,khd->hqk", query_all, key_own, preferred_element_type=jnp.float32)
        * score_scale
    )
    scores_k = jnp.where(own_live[None, None, :], scores_k, NEG_FILL)
    weights_k = jnp.exp(scores_k - log_total_all[:, :, None])
    value_acc = jnp.einsum(
        "hqk,qhd->khd", weights_k.astype(jnp.bfloat16), grad_all, preferred_element_type=jnp.float32
    )
    grad_weights_k = jnp.einsum(
        "qhd,khd->hqk", grad_all, value_own, preferred_element_type=jnp.float32
    )
    grad_scores_k = (weights_k * (grad_weights_k - row_delta_all[:, :, None]) * score_scale).astype(
        jnp.bfloat16
    )
    key_acc = jnp.einsum(
        "hqk,qhd->khd", grad_scores_k, query_all, preferred_element_type=jnp.float32
    )
    grad_queries = query_acc.reshape(1, frame_rows, flat_width).astype(jnp.bfloat16)
    grad_keys = key_acc.reshape(1, frame_rows, flat_width).astype(jnp.bfloat16)
    grad_values = value_acc.reshape(1, frame_rows, flat_width).astype(jnp.bfloat16)
    half_width = (KW - 1) // 2
    frame_ids = time_rank * frame_rows + jnp.arange(frame_rows, dtype=jnp.int32)
    frame_live = (frame_ids < length).astype(jnp.float32)[:, None]
    glu_rows = glu_input[0]
    linear = glu_rows[:, :CH].astype(jnp.float32)
    gate_sig = jax.nn.sigmoid(glu_rows[:, CH:].astype(jnp.float32))
    activ = (linear * gate_sig * frame_live).astype(jnp.bfloat16)
    padded = extended(activ, (("tm", 0),), half_width)
    kernel_f = full_kernel.astype(jnp.float32)
    gain_f = full_gain.astype(jnp.float32)
    mixed = depthwise(padded, kernel_f, frame_rows)
    grad_conv, gain_term = norm_backward(mixed, gain_f, conv_upstream[0], frame_live)
    grad_pad = extended(grad_conv, (("tm", 0),), half_width)
    kernel_term = tap_products(grad_conv, padded, frame_rows, KW)
    grad_activ = back_depthwise(grad_pad, kernel_f, frame_rows) * frame_live
    first_half = grad_activ * gate_sig
    second_half = grad_activ * linear * gate_sig * (1.0 - gate_sig)
    grad_glu = jnp.concatenate([first_half, second_half], axis=-1).astype(jnp.bfloat16)[None]
    attended_flat = attended.reshape(frame_rows, flat_width)
    proj_term = lax.dot_general(
        upstream_rows, attended_flat, (((0,), (0,)), ((), ())), preferred_element_type=jnp.float32
    )
    proj_total, kernel_total, gain_total = reduce_grads(proj_term, kernel_term, gain_term)
    grad_projection = proj_total.astype(jnp.bfloat16)
    return (
        grad_queries,
        grad_keys,
        grad_values,
        grad_projection,
        grad_glu,
        kernel_total,
        gain_total,
    )


def solution(mesh):
    in_specs = (
        P("dp", "tm", None),
        P("dp", "tm", None),
        P("dp", "tm", None),
        P("dp"),
        P("dp", None),
        P("dp", "tm", None),
        P("dp", "tm", None),
        P("dp", None),
        P("dp"),
        P("dp", "tm", None),
    )
    out_specs = (
        P("dp", "tm", None),
        P("dp", "tm", None),
        P("dp", "tm", None),
        P("dp", None),
        P("dp", "tm", None),
        P("dp", None),
        P("dp"),
    )
    return jax.shard_map(
        per_device, mesh=mesh, in_specs=in_specs, out_specs=out_specs, check_vma=False
    )
```

profile of v0, /device:TPU:4, one launch (start us, length us, event | category | flops | bytes accessed | tf_op | source)
XLA Modules:
  0.0 645.9 jit_solution(10095219337731439933)
XLA Ops:
  11.8 2.9 fusion.11
  18.0 5.2 collective-permute-start
  29.2 62.8 %all-gather.8.cloned.1.call-done = bf16[4352,256]{1,0:T(8,128)(2,1)} async-done(((bf16[136,256]{1,0:T(8,128)(2,1)}), bf16[4352,256]{1,0:T(8,128)(2,1)}) %all-gather.8.cloned.1.call-update) | async-done | bytes 2228240 | tf_op jit(solution)/shard_map/all_gather | solution.py:91
  95.2 19.6 %slice_reduce_fusion.30 = (f32[2048]{0:T(1024)S(1)}, f32[2048]{0:T(1024)S(1)}, f32[2048]{0:T(1024)S(1)}, f32[2048]{0:T(1024)S(1)}, f32[2048]{0:T(1024)S(1)}, /*i...) fusion(f32[2048,31]{1,0:T(8,128)} %reshape.264), kind=kLoop, calls=%fused_computation.353 | loop fusion | bytes 311296 | tf_op jit(solution)/shard_map/slice | solution.py:40
  114.9 6.6 %slice_reduce_fusion.29 = (f32[2048]{0:T(1024)S(1)}, f32[2048]{0:T(1024)S(1)}, f32[2048]{0:T(1024)S(1)}, f32[2048]{0:T(1024)S(1)}, f32[2048]{0:T(1024)S(1)}, /*i...) fusion(f32[2048,31]{1,0:T(8,128)S(1)} %copy-done.2), kind=kLoop, calls=%fused_computation.352 | loop fusion | bytes 196608 | tf_op jit(solution)/shard_map/slice | solution.py:40
  124.2 45.4 %fusion.185 = (f32[384]{0:T(512)S(1)}, f32[384,2048]{1,0:T(8,128)S(1)}) fusion(f32[2048]{0:T(1024)S(1)} %get-tuple-element.70, bf16[15,2048]{1,0:T(8,128)(2,1)} %collective-permute-done.1, bf16[384,2048]{1,0:T(8,128)(2,1)} %copy-done.4, f32[2048]{0:T(1024)S(1)} %get-tuple-element.71, f32[2048]{0:T(1024)S(1)} %get-tuple-element.72, ...), kind=kLoop, calls=%fused_computation.397 | loop fusion | flops 143916672 | bytes 5096960 | tf_op jit(solution)/shard_map/reduce_sum | solution.py:67
  170.2 3.9 multiply_reduce_fusion.1
  174.2 20.4 %fusion.75 = (f32[2048]{0:T(1024)}, f32[2048]{0:T(1024)}, f32[2048]{0:T(1024)}, f32[2048]{0:T(1024)}, f32[2048]{0:T(1024)}, /*index=5*/f32[2048]{0:T(1024)}, f32...) fusion(bf16[15,2048]{1,0:T(8,128)(2,1)} %collective-permute-done.1, ...), kind=kLoop, calls=%fused_computation.204 | loop fusion | flops 49526784 | bytes 9586688 | tf_op jit(solution)/shard_map/reduce_sum | solution.py:59
  194.6 4.2 fusion.58
  198.8 15.3 %fusion.74 = (f32[2048]{0:T(1024)S(1)}, f32[2048]{0:T(1024)S(1)}, f32[2048]{0:T(1024)S(1)}, f32[2048]{0:T(1024)S(1)}, f32[2048]{0:T(1024)S(1)}, /*index=5*/f32[2048]{0:T(1024)S(1)}, f32[2048]{0:T(1024)S(1)}) fusion(bf16[384,2048]{1,0:T(8,128)(2,1)S(1)} %get-tuple-element.102, bf16[15,2048]{1,0:T(8,128)(2,1)} %collective-permute-done.1, ...), kind=kLoop, calls=%fused_computation.203 | loop fusion | flops 31442944 | bytes 3264512 | tf_op jit(solution)/shard_map/reduce_sum | solution.py:59
  214.1 7.3 %fusion.59 = (f32[2048]{0:T(1024)S(1)}, f32[2048]{0:T(1024)}, f32[2048]{0:T(1024)}, f32[2048]{0:T(1024)}, f32[2048]{0:T(1024)}, /*index=5*/f32[2048]{0:T(1024)}, f32[2048]{0:T(1024)}, f32[2048]{0:T(1024)}, f32[2048]{0:T(1024)}) fusion(bf16[384,2048]{1,0:T(8,128)(2,1)S(1)} %get-tuple-element.102, bf16[384,2048]{1,0:T(8,128)(2,1)S(1)} %copy-done.5, ...), kind=kLoop, calls=%fused_computation.188 | loop fusion | flops 43235328 | bytes 3280896 | tf_op jit(solution)/shard_map/reduce_sum | solution.py:59
  221.4 3.4 stack.127
  242.5 3.2 fusion.7
  262.2 4.6 collective-permute-start.3
  268.0 3.3 convolution_bitcast_fusion
  273.5 33.0 %fusion.97 = (bf16[1,384,2048]{2,1,0:T(8,128)(2,1)S(1)}, f32[384,2048]{1,0:T(8,128)S(1)}) fusion(bf16[384,4096]{1,0:T(8,128)(2,1)} %bitcast.138, f32[384]{0:T(512)S(1)} %copy-done.86, f32[2048]{0:T(1024)S(1)} %copy-done.23, bf16[384,2048]{1,0:T(8,128)(2,1)S(1)} %copy-done.8, bf16[15,2048]{1,0:T(8,128)(2,1)} %collective-permute-done.3, ...), kind=kLoop, calls=%fused_computation.236 | loop fusion | flops 148635648 | bytes 8242688 | tf_op jit(solution)/shard_map/concatenate | solution.py:253
  309.7 36.1 %reduce-scatter.7.cloned.1.call-done = f32[8,256]{1,0:T(8,128)} async-done(((f32[256,256]{1,0:T(8,128)}), f32[8,256]{1,0:T(8,128)}) %reduce-scatter.7.cloned.1.call-update) | async-done | bytes 8208
  346.6 8.8 %fusion.158 = bf16[2,128,384]{2,1,0:T(8,128)(2,1)} fusion(bf16[3072,2,128]{0,2,1:T(8,128)(2,1)S(1)} %bitcast.142, bf16[384,2,128]{0,2,1:T(8,128)(2,1)S(1)} %bitcast.156, bf16[3072,2,128]{0,2,1:T(8,128)(2,1)S(1)} %bitcast.145, f32[2,3072,384]{2,1,0:T(8,128)} %copy-done.3, f32[2,384]{1,0:T(2,128)S(1)} %copy-done.84, f32[2,384]{1,0:T(2,128)S(1)} %log_add_fusion, ...), kind=kOutput, calls=%fused_computation.319 | convolution fusion | flops 1224572928 | bytes 12985344 | tf_op jit(solution)/shard_map/hqk,khd->qhd/dot_general | solution.py:192
  357.2 65.5 %all-gather.10.cloned.1.call-done = bf16[3200,512]{1,0:T(8,128)(2,1)} async-done(((bf16[400,512]{1,0:T(8,128)(2,1)}), bf16[3200,512]{1,0:T(8,128)(2,1)}) %all-gather.10.cloned.1.call-update) | async-done | bytes 3276816 | tf_op jit(solution)/shard_map/all_gather | solution.py:205
  431.7 5.2 fusion.169
  436.9 8.5 %fusion.157 = bf16[2,128,384]{2,1,0:T(8,128)(2,1)S(1)} fusion(bf16[3072,2,128]{0,2,1:T(8,128)(2,1)S(1)} %bitcast.147, f32[2,3072,384]{2,1,0:T(8,128)} %fusion.169, bf16[3072,2,128]{0,2,1:T(8,128)(2,1)S(1)} %bitcast.154, f32[2,3072]{1,0:T(2,128)S(1)} %bitcast.205, f32[2,3072]{1,0:T(2,128)S(1)} %bitcast.203, pred[384]{0:T(512)(128)(4,1)S(1)} %copy-done.88, ...), kind=kOutput, calls=%fused_computation.318 | convolution fusion | flops 1224572928 | bytes 13025664 | tf_op jit(solution)/shard_map/hqk,qhd->khd/dot_general | solution.py:230
  445.4 108.3 %reduce-scatter.5.cloned.1.call-done = f32[128,256]{0,1:T(8,128)} async-done(((f32[4096,256]{0,1:T(8,128)}), f32[128,256]{0,1:T(8,128)}) %reduce-scatter.5.cloned.1.call-update) | async-done | bytes 131088 | tf_op jit(solution)/shard_map/reduce_scatter | solution.py:105
  555.4 6.5 fusion.163
  563.5 71.1 %all-reduce.3.cloned.1.call-done = f32[136,256]{0,1:T(8,128)} async-done(((f32[136,256]{0,1:T(8,128)}), f32[136,256]{0,1:T(8,128)}) %all-reduce.3.cloned.1.call-update) | async-done | bytes 139280 | tf_op jit(solution)/shard_map/psum | solution.py:113
  (273 shorter events, 78.3 us)
Async XLA Ops:
  7.2 223.2 %copy-start = (bf16[1,384,4096]{2,1,0:T(8,128)(2,1)S(1)}, bf16[1,384,4096]{2,1,0:T(8,128)(2,1)}, u32[]{:S(2)}) copy-start(bf16[1,384,4096]{2,1,0:T(8,128)(2,1)} %param.15) | copy-start | bytes 9437188
  7.2 84.8 %all-gather.8.cloned.1.call-start = ((), (), s32[]{:S(2)}) async-start(), calls=%async_computation.5 | async-start | bytes 2297856 | tf_op jit(solution)/shard_map/all_gather | solution.py:91
  10.6 222.8 %all-gather.6.cloned.1.call-start = ((), (), s32[]{:S(2)}) async-start(), calls=%async_computation.2 | async-start | bytes 3538944 | tf_op jit(solution)/shard_map/all_gather | solution.py:159
  11.8 158.3 %copy-start.85 = (f32[384]{0:T(512)}, f32[384]{0:T(512)S(1)}, u32[]{:S(2)}) copy-start(f32[384]{0:T(512)S(1)} %get-tuple-element.106) | copy-start | bytes 4612
  16.7 107.3 %collective-permute-start.1 = (bf16[15,2048]{1,0:T(8,128)(2,1)}, bf16[15,2048]{1,0:T(8,128)(2,1)}, u32[]{:S(2)}, u32[]{:S(2)}) collective-permute-start(bf16[15,2048]{1,0:T(8,128)(2,1)} %get-tuple-element.115), channel_id=1, source_target_pairs={{1,0},{2,1},{3,2},{4,3},{5,4},{6,5},{7,6},{9,8},{10,9},{11,10},{12... | collective-permute-start | bytes 184328 | tf_op jit(solution)/shard_map/ppermute | solution.py:30
  18.0 106.0 %collective-permute-start = (bf16[15,2048]{1,0:T(8,128)(2,1)}, bf16[15,2048]{1,0:T(8,128)(2,1)}, u32[]{:S(2)}, u32[]{:S(2)}) collective-permute-start(bf16[15,2048]{1,0:T(8,128)(2,1)} %get-tuple-element.114), channel_id=1, source_target_pairs={{0,1},{1,2},{2,3},{3,4},{4,5},{5,6},{6,7},{8,9},{9,10},{10,11},{11... | collective-permute-start | bytes 184328 | tf_op jit(solution)/shard_map/ppermute | solution.py:28
  27.6 318.2 %reduce-scatter.7.cloned.1.call-start = ((), (), s32[]{:S(2)}) async-start(), calls=%async_computation.7 | async-start | bytes 270336
  121.5 48.1 %copy-start.58 = (f32[2048]{0:T(1024)}, f32[2048]{0:T(1024)S(1)}, u32[]{:S(2)}) copy-start(f32[2048]{0:T(1024)S(1)} %get-tuple-element.88) | copy-start | bytes 24580
  121.5 48.1 %copy-start.60 = (f32[2048]{0:T(1024)}, f32[2048]{0:T(1024)S(1)}, u32[]{:S(2)}) copy-start(f32[2048]{0:T(1024)S(1)} %get-tuple-element.89) | copy-start | bytes 24580
  121.5 48.1 %copy-start.62 = (f32[2048]{0:T(1024)}, f32[2048]{0:T(1024)S(1)}, u32[]{:S(2)}) copy-start(f32[2048]{0:T(1024)S(1)} %get-tuple-element.90) | copy-start | bytes 24580
  121.5 48.1 %copy-start.64 = (f32[2048]{0:T(1024)}, f32[2048]{0:T(1024)S(1)}, u32[]{:S(2)}) copy-start(f32[2048]{0:T(1024)S(1)} %get-tuple-element.91) | copy-start | bytes 24580
  121.6 48.1 %copy-start.66 = (f32[2048]{0:T(1024)}, f32[2048]{0:T(1024)S(1)}, u32[]{:S(2)}) copy-start(f32[2048]{0:T(1024)S(1)} %get-tuple-element.92) | copy-start | bytes 24580
  121.6 48.1 %copy-start.68 = (f32[2048]{0:T(1024)}, f32[2048]{0:T(1024)S(1)}, u32[]{:S(2)}) copy-start(f32[2048]{0:T(1024)S(1)} %get-tuple-element.93) | copy-start | bytes 24580
  121.6 48.1 %copy-start.70 = (f32[2048]{0:T(1024)}, f32[2048]{0:T(1024)S(1)}, u32[]{:S(2)}) copy-start(f32[2048]{0:T(1024)S(1)} %get-tuple-element.94) | copy-start | bytes 24580
  121.6 48.1 %copy-start.72 = (f32[2048]{0:T(1024)}, f32[2048]{0:T(1024)S(1)}, u32[]{:S(2)}) copy-start(f32[2048]{0:T(1024)S(1)} %get-tuple-element.95) | copy-start | bytes 24580
  121.6 48.1 %copy-start.74 = (f32[2048]{0:T(1024)}, f32[2048]{0:T(1024)S(1)}, u32[]{:S(2)}) copy-start(f32[2048]{0:T(1024)S(1)} %get-tuple-element.96) | copy-start | bytes 24580
  121.6 48.1 %copy-start.76 = (f32[2048]{0:T(1024)}, f32[2048]{0:T(1024)S(1)}, u32[]{:S(2)}) copy-start(f32[2048]{0:T(1024)S(1)} %get-tuple-element.97) | copy-start | bytes 24580
  121.6 48.1 %copy-start.78 = (f32[2048]{0:T(1024)}, f32[2048]{0:T(1024)S(1)}, u32[]{:S(2)}) copy-start(f32[2048]{0:T(1024)S(1)} %get-tuple-element.98) | copy-start | bytes 24580
  233.3 189.4 %all-gather.10.cloned.1.call-start = ((), (), s32[]{:S(2)}) async-start(), calls=%async_computation.6 | async-start | bytes 3686400 | tf_op jit(solution)/shard_map/all_gather | solution.py:205
  257.2 296.5 %reduce-scatter.5.cloned.1.call-start = ((), (), s32[]{:S(2)}) async-start(), calls=%async_computation.3 | async-start | bytes 4325376 | tf_op jit(solution)/shard_map/reduce_scatter | solution.py:105
  262.2 9.6 %collective-permute-start.3 = (bf16[15,2048]{1,0:T(8,128)(2,1)}, bf16[15,2048]{1,0:T(8,128)(2,1)}, u32[]{:S(2)}, u32[]{:S(2)}) collective-permute-start(bf16[15,2048]{1,0:T(8,128)(2,1)} %get-tuple-element.113), channel_id=1, source_target_pairs={{0,1},{1,2},{2,3},{3,4},{4,5},{5,6},{6,7},{8,9},{9,10},{10,11},{11... | collective-permute-start | bytes 184328 | tf_op jit(solution)/shard_map/ppermute | solution.py:28
  266.7 6.5 %collective-permute-start.2 = (bf16[15,2048]{1,0:T(8,128)(2,1)}, bf16[15,2048]{1,0:T(8,128)(2,1)}, u32[]{:S(2)}, u32[]{:S(2)}) collective-permute-start(bf16[15,2048]{1,0:T(8,128)(2,1)} %get-tuple-element.112), channel_id=1, source_target_pairs={{1,0},{2,1},{3,2},{4,3},{5,4},{6,5},{7,6},{9,8},{10,9},{11,10},{12... | collective-permute-start | bytes 184328 | tf_op jit(solution)/shard_map/ppermute | solution.py:30
  271.7 362.9 %all-reduce.3.cloned.1.call-start = ((), (), s32[]{:S(2)}) async-start(), calls=%async_computation.4 | async-start | bytes 524288 | tf_op jit(solution)/shard_map/psum | solution.py:113
  555.4 83.3 %copy-start.1 = (bf16[1,384,4096]{2,1,0:T(8,128)(2,1)S(1)}, bf16[1,384,4096]{2,1,0:T(8,128)(2,1)}, u32[]{:S(2)}) copy-start(bf16[1,384,4096]{2,1,0:T(8,128)(2,1)} %param.15) | copy-start | bytes 9437188
  (75 other events, 621.6 us)
Sparse Core Ops, SparseCore 0:
  11.3 80.6 all-gather.7
  93.8 73.0 all-gather.5
  233.4 112.3 reduce-scatter.6
  347.4 75.2 all-gather.9
  426.7 126.9 reduce-scatter.4
  556.2 78.3 all-reduce.2
where the time goes:
time: 658 us; the launch traced here: 646 us
  waiting for transfers between devices  345 us (52%)
  other arithmetic  151 us (23%)
  local copies, waits for them, and re-layouts  78.7 us (12%)
  matrix products  42 us (6%)
  between operations  16.7 us (3%)
  starting transfers between devices  12.6 us (2%)
    reduce_scatter x1, waiting for transfers between devices, reduce_grads(): lax.psum_scatter(proj_term, 'dp', scatter_dimension=0, tiled=True)  108 us
    psum x1, waiting for transfers between devices, reduce_grads(): total = lax.psum(jnp.concatenate([proj_part, tail_part], axis=0), 'tm')  71.1 us
    all_gather x1, waiting for transfers between devices, per_device(): query_grad = lax.all_gather(packed_rows, 'tm', axis=0, tiled=False)  65.5 us
    all_gather x1, waiting for transfers between devices, gather_params(): full = lax.all_gather(block, 'dp', axis=0, tiled=False)  62.8 us
    reduce_sum x4, other arithmetic, tap_products(): jnp.sum(grad_f * padded[tap:tap + frame_rows].astype(jnp.float32), axis=0)  47.2 us
    reduce_sum x1, other arithmetic, norm_backward(): centre = mixed - jnp.mean(mixed, axis=-1, keepdims=True)  45.4 us
    unnamed x7, waiting for transfers between devices  36.2 us
    concatenate x3, other arithmetic, per_device(): jnp.concatenate([first_half, second_half], axis=-1).astype(jnp.bfloat16)  36.1 us
  transfers between devices with their start and end apart: 10, of which 6 were waited for; matrix products, arithmetic and copies ran while one was open for 40% of the time, Pallas kernels for 0%

commit v1 on v0

--- a/solution.py
+++ b/solution.py
@@ -110,7 +110,7 @@
     tail_rows = -(-tail_cols // width)
     tail = jnp.pad(tail, ((0, 0), (0, tail_rows * width - tail_cols))).reshape(-1, width)
     tail_part = lax.psum_scatter(tail, "dp", scatter_dimension=0, tiled=True)
-    total = lax.psum(jnp.concatenate([proj_part, tail_part], axis=0), "tm")
+    total = jnp.sum(lax.all_gather(jnp.concatenate([proj_part, tail_part], axis=0), "tm"), axis=0)
     proj_rows = proj_part.shape[0]
     proj_total = total[:proj_rows]
     flat_tail = total[proj_rows:].reshape(-1)

time: 658 us -> 620 us (0.942)
  waiting for transfers between devices: 345 us -> 307 us
    psum x1 -> x0, waiting for transfers between devices: 71.1 us -> none  [reduce_grads(): total = lax.psum(jnp.concatenate([proj_part, tail_part], axis=0), 'tm')]
    all_gather x0 -> x1, waiting for transfers between devices: none -> 24.6 us  [reduce_grads(): lax.all_gather(jnp.concatenate([proj_part, tail_part], axis=0), 'tm')]
    reduce_scatter x1, waiting for transfers between devices: 108 us -> 116 us  [reduce_grads(): lax.psum_scatter(proj_term, 'dp', scatter_dimension=0, tiled=True)]
    unnamed x197 -> x195, local copies, waits for them, and re-layouts: 17 us -> 17.1 us
  transfers between devices with their start and end apart: 10 -> 10, of which waited for: 6 -> 6; matrix products, arithmetic and copies ran while one was open for 40% -> 43% of each run, Pallas kernels for 0% -> 0%
where the time goes in v1:
time: 620 us; the launch traced here: 608 us
  waiting for transfers between devices  307 us (50%)
  other arithmetic  152 us (25%)
  local copies, waits for them, and re-layouts  78.2 us (13%)
  matrix products  41.8 us (7%)
  between operations  16.7 us (3%)
  starting transfers between devices  12.6 us (2%)
    reduce_scatter x1, waiting for transfers between devices, reduce_grads(): lax.psum_scatter(proj_term, 'dp', scatter_dimension=0, tiled=True)  116 us
    all_gather x1, waiting for transfers between devices, per_device(): query_grad = lax.all_gather(packed_rows, 'tm', axis=0, tiled=False)  65.5 us
    all_gather x1, waiting for transfers between devices, gather_params(): full = lax.all_gather(block, 'dp', axis=0, tiled=False)  62.8 us
    reduce_sum x4, other arithmetic, tap_products(): jnp.sum(grad_f * padded[tap:tap + frame_rows].astype(jnp.float32), axis=0)  47.2 us
    reduce_sum x1, other arithmetic, norm_backward(): centre = mixed - jnp.mean(mixed, axis=-1, keepdims=True)  45.4 us
    unnamed x7, waiting for transfers between devices  36.2 us
    concatenate x3, other arithmetic, per_device(): jnp.concatenate([first_half, second_half], axis=-1).astype(jnp.bfloat16)  36.1 us
    slice x2, local copies, waits for them, and re-layouts, depthwise(): kernel_f[:, tap]  26.1 us
  transfers between devices with their start and end apart: 10, of which 6 were waited for; matrix products, arithmetic and copies ran while one was open for 43% of the time, Pallas kernels for 0%

profile of v1, /device:TPU:4, one launch (start us, length us, event | category | flops | bytes accessed | tf_op | source)
XLA Modules:
  0.0 608.0 jit_solution(5456365903199159374)
XLA Ops:
  11.8 2.9 fusion.11
  18.0 5.2 collective-permute-start
  29.2 62.8 %all-gather.10.cloned.1.call-done = bf16[4352,256]{1,0:T(8,128)(2,1)} async-done(((bf16[136,256]{1,0:T(8,128)(2,1)}), bf16[4352,256]{1,0:T(8,128)(2,1)}) %all-gather.10.cloned.1.call-update) | async-done | bytes 2228240 | tf_op jit(solution)/shard_map/all_gather | solution.py:91
  95.2 19.6 %slice_reduce_fusion.30 = (f32[2048]{0:T(1024)S(1)}, f32[2048]{0:T(1024)S(1)}, f32[2048]{0:T(1024)S(1)}, f32[2048]{0:T(1024)S(1)}, f32[2048]{0:T(1024)S(1)}, /*i...) fusion(f32[2048,31]{1,0:T(8,128)} %reshape.264), kind=kLoop, calls=%fused_computation.353 | loop fusion | bytes 311296 | tf_op jit(solution)/shard_map/slice | solution.py:40
  114.9 6.6 %slice_reduce_fusion.29 = (f32[2048]{0:T(1024)S(1)}, f32[2048]{0:T(1024)S(1)}, f32[2048]{0:T(1024)S(1)}, f32[2048]{0:T(1024)S(1)}, f32[2048]{0:T(1024)S(1)}, /*i...) fusion(f32[2048,31]{1,0:T(8,128)S(1)} %copy-done.2), kind=kLoop, calls=%fused_computation.352 | loop fusion | bytes 196608 | tf_op jit(solution)/shard_map/slice | solution.py:40
  124.2 45.4 %fusion.185 = (f32[384]{0:T(512)S(1)}, f32[384,2048]{1,0:T(8,128)S(1)}) fusion(f32[2048]{0:T(1024)S(1)} %get-tuple-element.70, bf16[15,2048]{1,0:T(8,128)(2,1)} %collective-permute-done.1, bf16[384,2048]{1,0:T(8,128)(2,1)} %copy-done.4, f32[2048]{0:T(1024)S(1)} %get-tuple-element.71, f32[2048]{0:T(1024)S(1)} %get-tuple-element.72, ...), kind=kLoop, calls=%fused_computation.398 | loop fusion | flops 143916672 | bytes 5096960 | tf_op jit(solution)/shard_map/reduce_sum | solution.py:67
  170.2 3.9 multiply_reduce_fusion.1
  174.2 20.4 %fusion.75 = (f32[2048]{0:T(1024)}, f32[2048]{0:T(1024)}, f32[2048]{0:T(1024)}, f32[2048]{0:T(1024)}, f32[2048]{0:T(1024)}, /*index=5*/f32[2048]{0:T(1024)}, f32...) fusion(bf16[15,2048]{1,0:T(8,128)(2,1)} %collective-permute-done.1, ...), kind=kLoop, calls=%fused_computation.204 | loop fusion | flops 49526784 | bytes 9586688 | tf_op jit(solution)/shard_map/reduce_sum | solution.py:59
  194.6 4.2 fusion.58
  198.8 15.3 %fusion.74 = (f32[2048]{0:T(1024)S(1)}, f32[2048]{0:T(1024)S(1)}, f32[2048]{0:T(1024)S(1)}, f32[2048]{0:T(1024)S(1)}, f32[2048]{0:T(1024)S(1)}, /*index=5*/f32[2048]{0:T(1024)S(1)}, f32[2048]{0:T(1024)S(1)}) fusion(bf16[384,2048]{1,0:T(8,128)(2,1)S(1)} %get-tuple-element.102, bf16[15,2048]{1,0:T(8,128)(2,1)} %collective-permute-done.1, ...), kind=kLoop, calls=%fused_computation.203 | loop fusion | flops 31442944 | bytes 3264512 | tf_op jit(solution)/shard_map/reduce_sum | solution.py:59
  214.1 7.3 %fusion.59 = (f32[2048]{0:T(1024)S(1)}, f32[2048]{0:T(1024)}, f32[2048]{0:T(1024)}, f32[2048]{0:T(1024)}, f32[2048]{0:T(1024)}, /*index=5*/f32[2048]{0:T(1024)}, f32[2048]{0:T(1024)}, f32[2048]{0:T(1024)}, f32[2048]{0:T(1024)}) fusion(bf16[384,2048]{1,0:T(8,128)(2,1)S(1)} %get-tuple-element.102, bf16[384,2048]{1,0:T(8,128)(2,1)S(1)} %copy-done.5, ...), kind=kLoop, calls=%fused_computation.188 | loop fusion | flops 43235328 | bytes 3280896 | tf_op jit(solution)/shard_map/reduce_sum | solution.py:59
  221.4 3.4 stack.127
  242.5 3.2 fusion.7
  262.2 4.6 collective-permute-start.3
  268.0 3.3 convolution_bitcast_fusion
  273.5 33.0 %fusion.97 = (bf16[1,384,2048]{2,1,0:T(8,128)(2,1)S(1)}, f32[384,2048]{1,0:T(8,128)S(1)}) fusion(bf16[384,4096]{1,0:T(8,128)(2,1)} %bitcast.140, f32[384]{0:T(512)S(1)} %copy-done.86, f32[2048]{0:T(1024)S(1)} %copy-done.23, bf16[384,2048]{1,0:T(8,128)(2,1)S(1)} %copy-done.8, bf16[15,2048]{1,0:T(8,128)(2,1)} %collective-permute-done.3, ...), kind=kLoop, calls=%fused_computation.236 | loop fusion | flops 148635648 | bytes 8242688 | tf_op jit(solution)/shard_map/concatenate | solution.py:253
  309.7 36.1 %reduce-scatter.7.cloned.1.call-done = f32[8,256]{1,0:T(8,128)} async-done(((f32[256,256]{1,0:T(8,128)}), f32[8,256]{1,0:T(8,128)}) %reduce-scatter.7.cloned.1.call-update) | async-done | bytes 8208
  346.6 8.8 %fusion.158 = bf16[2,128,384]{2,1,0:T(8,128)(2,1)} fusion(bf16[3072,2,128]{0,2,1:T(8,128)(2,1)S(1)} %bitcast.144, bf16[384,2,128]{0,2,1:T(8,128)(2,1)S(1)} %bitcast.159, bf16[3072,2,128]{0,2,1:T(8,128)(2,1)S(1)} %bitcast.147, f32[2,3072,384]{2,1,0:T(8,128)} %copy-done.3, f32[2,384]{1,0:T(2,128)S(1)} %copy-done.84, f32[2,384]{1,0:T(2,128)S(1)} %log_add_fusion, ...), kind=kOutput, calls=%fused_computation.319 | convolution fusion | flops 1224572928 | bytes 12985344 | tf_op jit(solution)/shard_map/hqk,khd->qhd/dot_general | solution.py:192
  357.2 65.5 %all-gather.12.cloned.1.call-done = bf16[3200,512]{1,0:T(8,128)(2,1)} async-done(((bf16[400,512]{1,0:T(8,128)(2,1)}), bf16[3200,512]{1,0:T(8,128)(2,1)}) %all-gather.12.cloned.1.call-update) | async-done | bytes 3276816 | tf_op jit(solution)/shard_map/all_gather | solution.py:205
  432.2 5.2 fusion.169
  437.4 116.3 %reduce-scatter.5.cloned.1.call-done = f32[128,256]{0,1:T(8,128)} async-done(((f32[4096,256]{0,1:T(8,128)}), f32[128,256]{0,1:T(8,128)}) %reduce-scatter.5.cloned.1.call-update) | async-done | bytes 131088 | tf_op jit(solution)/shard_map/reduce_scatter | solution.py:105
  556.2 8.3 %fusion.157 = bf16[2,128,384]{2,1,0:T(8,128)(2,1)S(1)} fusion(bf16[3072,2,128]{0,2,1:T(8,128)(2,1)S(1)} %bitcast.149, f32[2,3072,384]{2,1,0:T(8,128)} %fusion.169, bf16[3072,2,128]{0,2,1:T(8,128)(2,1)S(1)} %bitcast.156, f32[2,3072]{1,0:T(2,128)S(1)} %bitcast.207, f32[2,3072]{1,0:T(2,128)S(1)} %bitcast.205, pred[384]{0:T(512)(128)(4,1)S(1)} %copy-done.87, ...), kind=kOutput, calls=%fused_computation.318 | convolution fusion | flops 1224572928 | bytes 13025664 | tf_op jit(solution)/shard_map/hqk,qhd->khd/dot_general | solution.py:230
  565.4 6.5 %fusion.163 = bf16[2,128,384]{2,1,0:T(8,128)(2,1)S(1)} fusion(bf16[3072,2,128]{0,2,1:T(8,128)(2,1)} %bitcast.155, f32[2,3072,384]{2,1,0:T(8,128)} %fusion.169, f32[2,3072]{1,0:T(2,128)S(1)} %bitcast.206, pred[384]{0:T(512)(128)(4,1)S(1)} %copy-done.87), kind=kOutput, calls=%fused_computation.322 | convolution fusion | flops 613515264 | bytes 11231616 | tf_op jit(solution)/shard_map/hqk,qhd->khd/dot_general | solution.py:221
  572.7 24.6 %all-gather.14.cloned.1.call-done = f32[1088,256]{1,0:T(8,128)} async-done(((f32[136,256]{1,0:T(8,128)}), f32[1088,256]{1,0:T(8,128)}) %all-gather.14.cloned.1.call-update) | async-done | bytes 1114128 | tf_op jit(solution)/shard_map/all_gather | solution.py:113
  (271 shorter events, 79.0 us)
Async XLA Ops:
  7.2 223.2 %copy-start = (bf16[1,384,4096]{2,1,0:T(8,128)(2,1)S(1)}, bf16[1,384,4096]{2,1,0:T(8,128)(2,1)}, u32[]{:S(2)}) copy-start(bf16[1,384,4096]{2,1,0:T(8,128)(2,1)} %param.15) | copy-start | bytes 9437188
  7.2 84.8 %all-gather.10.cloned.1.call-start = ((), (), s32[]{:S(2)}) async-start(), calls=%async_computation.4 | async-start | bytes 2297856 | tf_op jit(solution)/shard_map/all_gather | solution.py:91
  10.6 222.8 %all-gather.8.cloned.1.call-start = ((), (), s32[]{:S(2)}) async-start(), calls=%async_computation.2 | async-start | bytes 3538944 | tf_op jit(solution)/shard_map/all_gather | solution.py:159
  11.8 158.3 %copy-start.85 = (f32[384]{0:T(512)}, f32[384]{0:T(512)S(1)}, u32[]{:S(2)}) copy-start(f32[384]{0:T(512)S(1)} %get-tuple-element.106) | copy-start | bytes 4612
  16.7 107.3 %collective-permute-start.1 = (bf16[15,2048]{1,0:T(8,128)(2,1)}, bf16[15,2048]{1,0:T(8,128)(2,1)}, u32[]{:S(2)}, u32[]{:S(2)}) collective-permute-start(bf16[15,2048]{1,0:T(8,128)(2,1)} %get-tuple-element.115), channel_id=1, source_target_pairs={{1,0},{2,1},{3,2},{4,3},{5,4},{6,5},{7,6},{9,8},{10,9},{11,10},{12... | collective-permute-start | bytes 184328 | tf_op jit(solution)/shard_map/ppermute | solution.py:30
  18.0 106.0 %collective-permute-start = (bf16[15,2048]{1,0:T(8,128)(2,1)}, bf16[15,2048]{1,0:T(8,128)(2,1)}, u32[]{:S(2)}, u32[]{:S(2)}) collective-permute-start(bf16[15,2048]{1,0:T(8,128)(2,1)} %get-tuple-element.114), channel_id=1, source_target_pairs={{0,1},{1,2},{2,3},{3,4},{4,5},{5,6},{6,7},{8,9},{9,10},{10,11},{11... | collective-permute-start | bytes 184328 | tf_op jit(solution)/shard_map/ppermute | solution.py:28
  27.6 318.2 %reduce-scatter.7.cloned.1.call-start = ((), (), s32[]{:S(2)}) async-start(), calls=%async_computation.7 | async-start | bytes 270336
  121.5 48.1 %copy-start.58 = (f32[2048]{0:T(1024)}, f32[2048]{0:T(1024)S(1)}, u32[]{:S(2)}) copy-start(f32[2048]{0:T(1024)S(1)} %get-tuple-element.88) | copy-start | bytes 24580
  121.5 48.1 %copy-start.60 = (f32[2048]{0:T(1024)}, f32[2048]{0:T(1024)S(1)}, u32[]{:S(2)}) copy-start(f32[2048]{0:T(1024)S(1)} %get-tuple-element.89) | copy-start | bytes 24580
  121.5 48.1 %copy-start.62 = (f32[2048]{0:T(1024)}, f32[2048]{0:T(1024)S(1)}, u32[]{:S(2)}) copy-start(f32[2048]{0:T(1024)S(1)} %get-tuple-element.90) | copy-start | bytes 24580
  121.5 48.1 %copy-start.64 = (f32[2048]{0:T(1024)}, f32[2048]{0:T(1024)S(1)}, u32[]{:S(2)}) copy-start(f32[2048]{0:T(1024)S(1)} %get-tuple-element.91) | copy-start | bytes 24580
  121.6 48.1 %copy-start.66 = (f32[2048]{0:T(1024)}, f32[2048]{0:T(1024)S(1)}, u32[]{:S(2)}) copy-start(f32[2048]{0:T(1024)S(1)} %get-tuple-element.92) | copy-start | bytes 24580
  121.6 48.1 %copy-start.68 = (f32[2048]{0:T(1024)}, f32[2048]{0:T(1024)S(1)}, u32[]{:S(2)}) copy-start(f32[2048]{0:T(1024)S(1)} %get-tuple-element.93) | copy-start | bytes 24580
  121.6 48.1 %copy-start.70 = (f32[2048]{0:T(1024)}, f32[2048]{0:T(1024)S(1)}, u32[]{:S(2)}) copy-start(f32[2048]{0:T(1024)S(1)} %get-tuple-element.94) | copy-start | bytes 24580
  121.6 48.1 %copy-start.72 = (f32[2048]{0:T(1024)}, f32[2048]{0:T(1024)S(1)}, u32[]{:S(2)}) copy-start(f32[2048]{0:T(1024)S(1)} %get-tuple-element.95) | copy-start | bytes 24580
  121.6 48.1 %copy-start.74 = (f32[2048]{0:T(1024)}, f32[2048]{0:T(1024)S(1)}, u32[]{:S(2)}) copy-start(f32[2048]{0:T(1024)S(1)} %get-tuple-element.96) | copy-start | bytes 24580
  121.6 48.1 %copy-start.76 = (f32[2048]{0:T(1024)}, f32[2048]{0:T(1024)S(1)}, u32[]{:S(2)}) copy-start(f32[2048]{0:T(1024)S(1)} %get-tuple-element.97) | copy-start | bytes 24580
  233.3 189.4 %all-gather.12.cloned.1.call-start = ((), (), s32[]{:S(2)}) async-start(), calls=%async_computation.5 | async-start | bytes 3686400 | tf_op jit(solution)/shard_map/all_gather | solution.py:205
  257.2 296.5 %reduce-scatter.5.cloned.1.call-start = ((), (), s32[]{:S(2)}) async-start(), calls=%async_computation.3 | async-start | bytes 4325376 | tf_op jit(solution)/shard_map/reduce_scatter | solution.py:105
  262.2 9.6 %collective-permute-start.3 = (bf16[15,2048]{1,0:T(8,128)(2,1)}, bf16[15,2048]{1,0:T(8,128)(2,1)}, u32[]{:S(2)}, u32[]{:S(2)}) collective-permute-start(bf16[15,2048]{1,0:T(8,128)(2,1)} %get-tuple-element.113), channel_id=1, source_target_pairs={{0,1},{1,2},{2,3},{3,4},{4,5},{5,6},{6,7},{8,9},{9,10},{10,11},{11... | collective-permute-start | bytes 184328 | tf_op jit(solution)/shard_map/ppermute | solution.py:28
  266.7 6.5 %collective-permute-start.2 = (bf16[15,2048]{1,0:T(8,128)(2,1)}, bf16[15,2048]{1,0:T(8,128)(2,1)}, u32[]{:S(2)}, u32[]{:S(2)}) collective-permute-start(bf16[15,2048]{1,0:T(8,128)(2,1)} %get-tuple-element.112), channel_id=1, source_target_pairs={{1,0},{2,1},{3,2},{4,3},{5,4},{6,5},{7,6},{9,8},{10,9},{11,10},{12... | collective-permute-start | bytes 184328 | tf_op jit(solution)/shard_map/ppermute | solution.py:30
  271.7 325.6 %all-gather.14.cloned.1.call-start = ((), (), s32[]{:S(2)}) async-start(), calls=%async_computation.6 | async-start | bytes 1253376 | tf_op jit(solution)/shard_map/all_gather | solution.py:113
  432.2 124.0 %copy-start.17 = (bf16[3072,256]{0,1:T(8,128)(2,1)S(1)}, bf16[3072,256]{0,1:T(8,128)(2,1)}, u32[]{:S(2)}) copy-start(bf16[3072,256]{0,1:T(8,128)(2,1)} %copy.124) | copy-start | bytes 4718596
  432.2 124.0 %copy-start.87 = (pred[384]{0:T(512)(128)(4,1)S(1)}, pred[384]{0:T(512)(128)(4,1)}, u32[]{:S(2)}) copy-start(pred[384]{0:T(512)(128)(4,1)} %get-tuple-element.107) | copy-start | bytes 1156
  (74 other events, 689.9 us)
Sparse Core Ops, SparseCore 0:
  11.3 80.6 all-gather.9
  93.8 73.0 all-gather.7
  233.4 112.3 reduce-scatter.6
  347.4 75.2 all-gather.11
  426.7 126.9 reduce-scatter.4
  555.5 41.6 all-gather.13
